TPU v7x, 256 devices: a whole 4x4x8 slice. The times are simulated.
256 devices in a mesh: row: 8 (over z_lo, y), col: 32 (over z_hi, x, core).
Axes of the slice: x: 4, y: 4, z: 8 (z_hi: 4, z_lo: 2; z = z_hi * 2 + z_lo), core: 2. Of those that a mesh axis runs over, the one named last changes fastest.
Arguments:
- strip: float32 [12, 2048, 2, 1024], P(None, 'col', None, 'row'), may hold values from -6 to 6
- lower: float32 [12, 2048, 2, 1024], P(None, 'col', None, 'row'), may hold values from -1.6 to 1.6, as said below
Outputs:
- reduced: float32 [12, 2048, 2, 1024], P(None, 'col', None, 'row')
Inputs may be any that keep to these rules, and one draw needn't show every extreme that they name: `lower`: in the first 2048 rows the diagonal lies between 0.8 and 1.6 and entries above it are zero.
All inputs are finite; a program needn't handle non-finite values.
Results may differ from a plain program's by a relative error of at most 0.00013.
Values sent between devices are 32-bit elements; how exact they have to be, the bound alone decides.
No kernel may reach another device: no remote copies, remote signals or barrier semaphores. Data moves between devices by JAX's collectives and lax.ppermute only.
A program may use at most 64 MiB of HBM per device.

v0:
```python
import jax
import jax.numpy as jnp
from jax import lax
from jax.sharding import PartitionSpec as P

highest = lax.Precision.HIGHEST


def spread(array, axis, root):
    mine = lax.axis_index(axis) == root
    return lax.psum(jnp.where(mine, array, jnp.zeros_like(array)), axis)


def times_rows(coeff, right_side):
    return jnp.dot(coeff, right_side, precision=highest, preferred_element_type=jnp.float32)


def times_rows_turned(coeff, right_turned):
    return lax.dot_general(
        coeff,
        right_turned,
        (((1,), (1,)), ((), ())),
        precision=highest,
        preferred_element_type=jnp.float32,
    )


def local(strip, lower):
    rounds = strip.shape[0]
    strip_width = strip.shape[1]
    row_run = strip.shape[3]
    row_count = lax.axis_size("row")
    block_size = row_run * row_count
    cols_here = rounds * strip_width
    trail_count = cols_here - strip_width
    local_strip = strip.reshape(cols_here, 2, row_run)
    left_part = local_strip[:, 0, :]
    right_part = local_strip[:, 1, :]
    gathered = lax.all_gather(lower[0], "col", axis=0, tiled=True)
    first_cols = gathered[:block_size, 0, :]
    cross_cols = gathered[block_size:, 0, :]
    second_cols = gathered[block_size:, 1, :]
    inverse_all = lax.all_gather(second_cols, "row", axis=1, tiled=True)
    mixed_cols = jnp.dot(
        inverse_all, cross_cols, precision=highest, preferred_element_type=jnp.float32
    )
    upper_half = lax.psum_scatter(
        times_rows_turned(first_cols, left_part), "row", scatter_dimension=0, tiled=True
    )
    carried = lax.psum_scatter(
        times_rows(cross_cols, upper_half), "row", scatter_dimension=0, tiled=True
    )
    remainder = right_part.T - carried
    lower_half = lax.psum_scatter(
        times_rows(second_cols, remainder), "row", scatter_dimension=0, tiled=True
    )
    solved = jnp.stack([upper_half.T, lower_half.T], axis=1)
    lead_rows = solved[:strip_width].reshape(strip_width, 2 * row_run)
    tail_rows = solved[strip_width:].reshape(trail_count, 2 * row_run)
    col_position = lax.axis_index("col")
    offset = col_position * strip_width
    part_block = offset // block_size
    inside = offset % block_size
    root_row = inside // row_run
    shift_in = inside % row_run
    zero_index = jnp.zeros((), jnp.int32)
    mirror_piece = lax.dynamic_slice(
        gathered, (zero_index, part_block, shift_in), (2 * block_size, 1, strip_width)
    )
    mirror_piece = mirror_piece.reshape(2 * block_size, strip_width)
    mirrored = spread(mirror_piece, "row", root_row)
    first_flag = (part_block == 0).astype(jnp.float32)
    second_flag = 1.0 - first_flag
    row_position = lax.axis_index("row")
    first_rows = lax.dynamic_slice_in_dim(mirrored, row_position * row_run, row_run, 0)
    partial_mix = jnp.dot(
        mixed_cols, first_rows, precision=highest, preferred_element_type=jnp.float32
    )
    chained = lax.psum(partial_mix, "row")
    coeff_whole = jnp.concatenate(
        [
            first_flag * mirrored[:block_size],
            second_flag * mirrored[block_size:] - first_flag * chained,
        ],
        axis=0,
    )
    solved_lead = lax.psum_scatter(
        times_rows(coeff_whole, lead_rows), "col", scatter_dimension=0, tiled=True
    )
    everything = lax.all_gather(solved_lead, "col", axis=0, tiled=True)
    left_rows = lower[1:].reshape(trail_count, 2 * row_run)
    grouped = everything.reshape(2, row_count, row_run, 2 * row_run).transpose(1, 0, 2, 3)
    swapped = lax.all_to_all(grouped, "row", split_axis=0, concat_axis=0, tiled=True)
    turned_block = swapped.reshape(row_count, 2, row_run, 2, row_run).transpose(0, 3, 4, 1, 2)
    turned_block = turned_block.reshape(row_count * 2 * row_run, 2 * row_run)
    summed = lax.psum_scatter(
        times_rows_turned(turned_block, left_rows), "row", scatter_dimension=0, tiled=True
    )
    update = summed.T
    reduced = jnp.concatenate([solved_lead, tail_rows - update], axis=0)
    return reduced.reshape(rounds, strip_width, 2, row_run)


def solution(mesh):
    in_specs = (P(None, "col", None, "row"), P(None, "col", None, "row"))
    out_specs = P(None, "col", None, "row")
    return jax.shard_map(local, mesh=mesh, in_specs=in_specs, out_specs=out_specs, check_vma=False)
```

profile of v0, /device:TPU:1, one launch (start us, length us, event | category | flops | bytes accessed | tf_op | source)
XLA Modules:
  0.0 760.2 jit_solution(14494232658817926773)
XLA Ops:
  6.5 1.5 slice_bitcast_fusion.3
  8.1 1.2 copy.10
  9.3 59.5 %all-gather.8.cloned.1.call-done = f32[1,2048,2,128]{3,2,0,1:T(2,128)} async-done(((f32[1,64,2,128]{3,2,0,1:T(2,128)}), f32[1,2048,2,128]{3,2,0,1:T(2,128)}) %all-gather.8.cloned.1.call-update) | async-done | bytes 2097168 | tf_op jit(solution)/shard_map/all_gather | solution.py:39
  68.8 4.1 fusion.20
  73.0 4.3 fusion.14
  77.4 0.7 all-gather.10.cloned.1.call-update
  78.2 3.5 constant_dynamic-slice_fusion
  82.3 0.9 select_bitcast_fusion
  83.3 35.7 %reduce-scatter.6.cloned.1.call-done = f32[128,768]{1,0:T(8,128)} async-done(((f32[1024,768]{1,0:T(8,128)}), f32[128,768]{1,0:T(8,128)}) %reduce-scatter.6.cloned.1.call-update) | async-done | bytes 393232 | tf_op jit(solution)/shard_map/reduce_scatter | solution.py:47
  118.9 5.3 convolution_bitcast_fusion.1
  124.3 97.1 %all-gather.10.cloned.1.call-done = f32[1024,1,1024]{2,1,0:T(1,128)} async-done(((f32[1024,1,128]{2,1,0:T(1,128)}), f32[1024,1,1024]{2,1,0:T(1,128)}) %all-gather.10.cloned.1.call-update) | async-done | bytes 4194320 | tf_op jit(solution)/shard_map/all_gather | solution.py:43
  221.5 5.7 fusion
  227.2 74.9 %all-reduce.3.cloned.1.call-done = f32[2048,64]{0,1:T(8,128)} async-done(((f32[2048,64]{0,1:T(8,128)}), f32[2048,64]{0,1:T(8,128)}) %all-reduce.3.cloned.1.call-update) | async-done | bytes 524304 | tf_op jit(solution)/shard_map/psum | solution.py:11
  302.1 2.2 fusion.16
  304.5 49.9 %reduce-scatter.8.cloned.1.call-done = f32[128,768]{0,1:T(8,128)} async-done(((f32[1024,768]{0,1:T(8,128)}), f32[128,768]{0,1:T(8,128)}) %reduce-scatter.8.cloned.1.call-update) | async-done | bytes 393232 | tf_op jit(solution)/shard_map/reduce_scatter | solution.py:50
  354.4 5.3 convolution_bitcast_fusion
  359.8 74.5 %all-reduce.5.cloned.1.call-done = f32[1024,64]{0,1:T(8,128)} async-done(((f32[1024,64]{0,1:T(8,128)}), f32[1024,64]{0,1:T(8,128)}) %all-reduce.5.cloned.1.call-update) | async-done | bytes 262160 | tf_op jit(solution)/shard_map/psum | solution.py:79
  434.3 1.0 slice_multiply_fusion.1
  435.3 50.9 %reduce-scatter.10.cloned.1.call-done = f32[128,768]{1,0:T(8,128)} async-done(((f32[1024,768]{1,0:T(8,128)}), f32[128,768]{1,0:T(8,128)}) %reduce-scatter.10.cloned.1.call-update) | async-done | bytes 393232 | tf_op jit(solution)/shard_map/reduce_scatter | solution.py:54
  486.2 0.8 pad_maximum_fusion.2
  487.0 3.2 fusion.8
  490.3 92.9 %reduce-scatter.12.cloned.1.call-done = f32[64,256]{1,0:T(8,128)} async-done(((f32[2048,256]{1,0:T(8,128)}), f32[64,256]{1,0:T(8,128)}) %reduce-scatter.12.cloned.1.call-update) | async-done | bytes 65552 | tf_op jit(solution)/shard_map/reduce_scatter | solution.py:87
  583.2 57.3 %all-gather.6.cloned.1.call-done = f32[2048,256]{1,0:T(8,128)} async-done(((f32[64,256]{1,0:T(8,128)}), f32[2048,256]{1,0:T(8,128)}) %all-gather.6.cloned.1.call-update) | async-done | bytes 2097168 | tf_op jit(solution)/shard_map/all_gather | solution.py:90
  640.5 3.1 copy.35
  643.6 4.3 all-to-all-start
  648.0 26.2 %all-to-all-done = f32[8,2,128,256]{3,2,1,0:T(8,128)} async-done(((f32[8,2,128,256]{3,2,1,0:T(8,128)}), f32[8,2,128,256]{3,2,1,0:T(8,128)}, u32[]{:S(2)}, u32[]{:S(2)}) %all-to-all-start) | async-done | bytes 2097184 | tf_op jit(solution)/shard_map/all_to_all | solution.py:93
  674.2 2.8 copy.16
  677.1 6.8 fusion.3
  683.9 1.0 copy-done.2
  685.4 65.5 %reduce-scatter.14.cloned.1.call-done = f32[256,704]{0,1:T(8,128)} async-done(((f32[2048,704]{0,1:T(8,128)}), f32[256,704]{0,1:T(8,128)}) %reduce-scatter.14.cloned.1.call-update) | async-done | bytes 720912 | tf_op jit(solution)/shard_map/reduce_scatter | solution.py:96
  750.9 1.2 bitcast_subtract_fusion
  752.1 1.3 reshape.35
  (34 shorter events, 1.9 us)
Async XLA Ops:
  6.5 62.3 %all-gather.8.cloned.1.call-start = ((), (), s32[]{:S(2)}) async-start(), calls=%async_computation.14 | async-start | bytes 2162688 | tf_op jit(solution)/shard_map/all_gather | solution.py:39
  8.0 110.9 %reduce-scatter.6.cloned.1.call-start = ((), (), s32[]{:S(2)}) async-start(), calls=%async_computation.8 | async-start | bytes 3538944 | tf_op jit(solution)/shard_map/reduce_scatter | solution.py:47
  77.3 144.2 %all-gather.10.cloned.1.call-start = ((), (), s32[]{:S(2)}) async-start(), calls=%async_computation.15 | async-start | bytes 4718592 | tf_op jit(solution)/shard_map/all_gather | solution.py:43
  78.0 224.0 %all-reduce.3.cloned.1.call-start = ((), (), s32[]{:S(2)}) async-start(), calls=%async_computation.6 | async-start | bytes 1048576 | tf_op jit(solution)/shard_map/psum | solution.py:11
  83.2 271.2 %reduce-scatter.8.cloned.1.call-start = ((), (), s32[]{:S(2)}) async-start(), calls=%async_computation.9 | async-start | bytes 3538944 | tf_op jit(solution)/shard_map/reduce_scatter | solution.py:50
  124.3 310.0 %all-reduce.5.cloned.1.call-start = ((), (), s32[]{:S(2)}) async-start(), calls=%async_computation.7 | async-start | bytes 524288 | tf_op jit(solution)/shard_map/psum | solution.py:79
  124.3 230.0 %copy-start = (f32[1024,1,128]{2,1,0:T(1,128)S(1)}, f32[1024,1,128]{2,1,0:T(1,128)}, u32[]{:S(2)}) copy-start(f32[1024,1,128]{2,1,0:T(1,128)} %get-tuple-element.6) | copy-start | bytes 1572868
  304.3 181.9 %reduce-scatter.10.cloned.1.call-start = ((), (), s32[]{:S(2)}) async-start(), calls=%async_computation.10 | async-start | bytes 3538944 | tf_op jit(solution)/shard_map/reduce_scatter | solution.py:54
  354.4 79.9 %copy-start.3 = (f32[2048,64]{0,1:T(8,128)S(1)}, f32[2048,64]{0,1:T(8,128)}, u32[]{:S(2)}) copy-start(f32[2048,64]{0,1:T(8,128)} %all-reduce.3.cloned.1.call-done) | copy-start | bytes 1572868
  359.7 126.5 %copy-start.1 = (f32[128,768]{1,0:T(8,128)S(1)}, f32[128,768]{1,0:T(8,128)}, u32[]{:S(2)}) copy-start(f32[128,768]{1,0:T(8,128)} %reduce-scatter.6.cloned.1.call-done) | copy-start | bytes 1179652
  359.8 223.5 %reduce-scatter.12.cloned.1.call-start = ((), (), s32[]{:S(2)}) async-start(), calls=%async_computation.11 | async-start | bytes 2162688 | tf_op jit(solution)/shard_map/reduce_scatter | solution.py:87
  490.2 150.3 %all-gather.6.cloned.1.call-start = ((), (), s32[]{:S(2)}) async-start(), calls=%async_computation.12 | async-start | bytes 2162688 | tf_op jit(solution)/shard_map/all_gather | solution.py:90
  643.6 30.6 %all-to-all-start = ((f32[8,2,128,256]{3,2,1,0:T(8,128)}), f32[8,2,128,256]{3,2,1,0:T(8,128)}, u32[]{:S(2)}, u32[]{:S(2)}) async-start(f32[8,2,128,256]{3,2,1,0:T(8,128)} %bitcast.59), calls=%async_computation.4 | async-start | bytes 4194304 | tf_op jit(solution)/shard_map/all_to_all | solution.py:93
  648.0 29.1 %slice-start = ((f32[12,64,2,128]{3,2,1,0:T(2,128)}), f32[11,64,2,128]{3,2,1,0:T(2,128)S(1)}, s32[]{:S(2)}) async-start(f32[12,64,2,128]{3,2,1,0:T(2,128)} %param.3), calls=%async_computation.16 | async-start | bytes 1441792 | tf_op jit(solution)/shard_map/slice | solution.py:91
  648.0 102.9 %reduce-scatter.14.cloned.1.call-start = ((), (), s32[]{:S(2)}) async-start(), calls=%async_computation.13 | async-start | bytes 6488064 | tf_op jit(solution)/shard_map/reduce_scatter | solution.py:96
  683.8 1.0 copy-start.2
  684.8 67.2 %copy-start.4 = (f32[64,256]{1,0:T(8,128)S(1)}, f32[64,256]{1,0:T(8,128)}, u32[]{:S(2)}) copy-start(f32[64,256]{1,0:T(8,128)} %reduce-scatter.12.cloned.1.call-done) | copy-start | bytes 196612
Sparse Core Ops, SparseCore 0:
  9.9 58.8 all-gather.7
  77.4 41.4 reduce-scatter.5
  120.6 100.7 all-gather.9
  224.0 78.0 all-reduce.2
  304.7 49.6 reduce-scatter.7
  357.0 77.2 all-reduce.4
  436.8 49.2 reduce-scatter.9
  490.4 92.8 reduce-scatter.11
  585.8 54.6 all-gather.5
  684.0 66.8 reduce-scatter.13
where the time goes:
time: 761 us; the launch traced here: 760 us
  waiting for transfers between devices  685 us (90%)
  matrix products  32.9 us (4%)
  local copies, waits for them, and re-layouts  19.4 us (3%)
  between operations  13.7 us (2%)
    all_gather x1, waiting for transfers between devices, local(): inverse_all = lax.all_gather(second_cols, 'row', axis=1, tiled=True)  97.1 us
    reduce_scatter x1, waiting for transfers between devices, local(): lax.psum_scatter(times_rows(coeff_whole, lead_rows), 'col', scatter_dimen...  92.9 us
    psum x1, waiting for transfers between devices, spread(): return lax.psum(jnp.where(mine, array, jnp.zeros_like(array)), axis)  74.9 us
    psum x1, waiting for transfers between devices, local(): chained = lax.psum(partial_mix, 'row')  74.5 us
    reduce_scatter x1, waiting for transfers between devices, local(): lax.psum_scatter(times_rows_turned(turned_block, left_rows), 'row', scatt...  65.5 us
    all_gather x1, waiting for transfers between devices, local(): gathered = lax.all_gather(lower[0], 'col', axis=0, tiled=True)  59.5 us
    all_gather x1, waiting for transfers between devices, local(): everything = lax.all_gather(solved_lead, 'col', axis=0, tiled=True)  57.3 us
    reduce_scatter x1, waiting for transfers between devices, local(): lax.psum_scatter(times_rows(second_cols, remainder), 'row', scatter_dimen...  50.9 us
  transfers between devices with their start and end apart: 11, of which 11 were waited for; matrix products, arithmetic and copies ran while one was open for 3% of the time, Pallas kernels for 0%

commit v1 on v0

--- a/solution.py
+++ b/solution.py
@@ -76,7 +76,8 @@
     partial_mix = jnp.dot(
         mixed_cols, first_rows, precision=highest, preferred_element_type=jnp.float32
     )
-    chained = lax.psum(partial_mix, "row")
+    parts = lax.all_gather(partial_mix, "row", axis=0, tiled=False)
+    chained = parts.sum(axis=0)
     coeff_whole = jnp.concatenate(
         [
             first_flag * mirrored[:block_size],

time: 761 us -> 725 us (0.953)
  waiting for transfers between devices: 685 us -> 647 us
    psum x1 -> x0, waiting for transfers between devices: 74.5 us -> none  [local(): chained = lax.psum(partial_mix, 'row')]
    all_gather x0 -> x1, waiting for transfers between devices: none -> 38.7 us  [local(): parts = lax.all_gather(partial_mix, 'row', axis=0, tiled=False)]
  transfers between devices with their start and end apart: 11 -> 11, of which waited for: 11 -> 11; matrix products, arithmetic and copies ran while one was open for 3% -> 4% of each run, Pallas kernels for 0% -> 0%
where the time goes in v1:
time: 725 us
  waiting for transfers between devices  647 us (89%)
  matrix products  32.8 us (5%)
  local copies, waits for them, and re-layouts  22.7 us (3%)
  between operations  13.8 us (2%)
    all_gather x1, waiting for transfers between devices, local(): inverse_all = lax.all_gather(second_cols, 'row', axis=1, tiled=True)  97.1 us
    reduce_scatter x1, waiting for transfers between devices, local(): lax.psum_scatter(times_rows(coeff_whole, lead_rows), 'col', scatter_dimen...  93.2 us
    psum x1, waiting for transfers between devices, spread(): return lax.psum(jnp.where(mine, array, jnp.zeros_like(array)), axis)  74.9 us
    reduce_scatter x1, waiting for transfers between devices, local(): lax.psum_scatter(times_rows_turned(turned_block, left_rows), 'row', scatt...  65.5 us
    all_gather x1, waiting for transfers between devices, local(): gathered = lax.all_gather(lower[0], 'col', axis=0, tiled=True)  59.5 us
    all_gather x1, waiting for transfers between devices, local(): everything = lax.all_gather(solved_lead, 'col', axis=0, tiled=True)  57.5 us
    reduce_scatter x1, waiting for transfers between devices, local(): lax.psum_scatter(times_rows(cross_cols, upper_half), 'row', scatter_dimen...  49.9 us
    reduce_scatter x1, waiting for transfers between devices, local(): lax.psum_scatter(times_rows(second_cols, remainder), 'row', scatter_dimen...  47.8 us
  transfers between devices with their start and end apart: 11, of which 11 were waited for; matrix products, arithmetic and copies ran while one was open for 4% of the time, Pallas kernels for 0%

profile of v1, /device:TPU:1, one launch (start us, length us, event | category | flops | bytes accessed | tf_op | source)
XLA Modules:
  0.0 724.8 jit_solution(7264689366832184464)
XLA Ops:
  6.5 1.5 slice_bitcast_fusion.3
  8.1 1.2 copy.10
  9.3 59.5 %all-gather.10.cloned.1.call-done = f32[1,2048,2,128]{3,2,0,1:T(2,128)} async-done(((f32[1,64,2,128]{3,2,0,1:T(2,128)}), f32[1,2048,2,128]{3,2,0,1:T(2,128)}) %all-gather.10.cloned.1.call-update) | async-done | bytes 2097168 | tf_op jit(solution)/shard_map/all_gather | solution.py:39
  68.8 4.1 fusion.20
  73.0 4.3 fusion.14
  77.4 0.7 all-gather.12.cloned.1.call-update
  78.2 3.5 constant_dynamic-slice_fusion
  82.3 0.9 select_bitcast_fusion
  83.2 35.7 %reduce-scatter.6.cloned.1.call-done = f32[128,768]{1,0:T(8,128)} async-done(((f32[1024,768]{1,0:T(8,128)}), f32[128,768]{1,0:T(8,128)}) %reduce-scatter.6.cloned.1.call-update) | async-done | bytes 393232 | tf_op jit(solution)/shard_map/reduce_scatter | solution.py:47
  118.9 5.3 convolution_bitcast_fusion.1
  124.3 97.1 %all-gather.12.cloned.1.call-done = f32[1024,1,1024]{2,1,0:T(1,128)} async-done(((f32[1024,1,128]{2,1,0:T(1,128)}), f32[1024,1,1024]{2,1,0:T(1,128)}) %all-gather.12.cloned.1.call-update) | async-done | bytes 4194320 | tf_op jit(solution)/shard_map/all_gather | solution.py:43
  221.5 5.7 fusion
  227.2 74.9 %all-reduce.2.cloned.1.call-done = f32[2048,64]{0,1:T(8,128)} async-done(((f32[2048,64]{0,1:T(8,128)}), f32[2048,64]{0,1:T(8,128)}) %all-reduce.2.cloned.1.call-update) | async-done | bytes 524304 | tf_op jit(solution)/shard_map/psum | solution.py:11
  302.1 2.2 fusion.16
  304.5 49.9 %reduce-scatter.8.cloned.1.call-done = f32[128,768]{0,1:T(8,128)} async-done(((f32[1024,768]{0,1:T(8,128)}), f32[128,768]{0,1:T(8,128)}) %reduce-scatter.8.cloned.1.call-update) | async-done | bytes 393232 | tf_op jit(solution)/shard_map/reduce_scatter | solution.py:50
  354.4 5.3 convolution_bitcast_fusion
  359.7 38.7 %all-gather.14.cloned.1.call-done = f32[8192,64]{0,1:T(8,128)} async-done(((f32[1024,64]{0,1:T(8,128)}), f32[8192,64]{0,1:T(8,128)}) %all-gather.14.cloned.1.call-update) | async-done | bytes 2097168 | tf_op jit(solution)/shard_map/all_gather | solution.py:79
  398.4 2.8 copy.20
  402.3 47.8 %reduce-scatter.10.cloned.1.call-done = f32[128,768]{1,0:T(8,128)} async-done(((f32[1024,768]{1,0:T(8,128)}), f32[128,768]{1,0:T(8,128)}) %reduce-scatter.10.cloned.1.call-update) | async-done | bytes 393232 | tf_op jit(solution)/shard_map/reduce_scatter | solution.py:54
  450.1 0.8 pad_maximum_fusion.2
  451.0 3.2 fusion.8
  454.2 93.2 %reduce-scatter.12.cloned.1.call-done = f32[64,256]{1,0:T(8,128)} async-done(((f32[2048,256]{1,0:T(8,128)}), f32[64,256]{1,0:T(8,128)}) %reduce-scatter.12.cloned.1.call-update) | async-done | bytes 65552 | tf_op jit(solution)/shard_map/reduce_scatter | solution.py:88
  547.5 57.5 %all-gather.8.cloned.1.call-done = f32[2048,256]{1,0:T(8,128)} async-done(((f32[64,256]{1,0:T(8,128)}), f32[2048,256]{1,0:T(8,128)}) %all-gather.8.cloned.1.call-update) | async-done | bytes 2097168 | tf_op jit(solution)/shard_map/all_gather | solution.py:91
  605.0 3.1 copy.36
  608.1 4.3 all-to-all-start
  612.5 26.2 %all-to-all-done = f32[8,2,128,256]{3,2,1,0:T(8,128)} async-done(((f32[8,2,128,256]{3,2,1,0:T(8,128)}), f32[8,2,128,256]{3,2,1,0:T(8,128)}, u32[]{:S(2)}, u32[]{:S(2)}) %all-to-all-start) | async-done | bytes 2097184 | tf_op jit(solution)/shard_map/all_to_all | solution.py:94
  638.7 2.8 copy.16
  641.6 6.8 fusion.3
  648.4 1.0 copy-done.2
  649.9 65.5 %reduce-scatter.14.cloned.1.call-done = f32[256,704]{0,1:T(8,128)} async-done(((f32[2048,704]{0,1:T(8,128)}), f32[256,704]{0,1:T(8,128)}) %reduce-scatter.14.cloned.1.call-update) | async-done | bytes 720912 | tf_op jit(solution)/shard_map/reduce_scatter | solution.py:97
  715.4 1.2 bitcast_subtract_fusion
  716.7 1.3 reshape.35
  (36 shorter events, 3.0 us)
Async XLA Ops:
  6.5 62.3 %all-gather.10.cloned.1.call-start = ((), (), s32[]{:S(2)}) async-start(), calls=%async_computation.13 | async-start | bytes 2162688 | tf_op jit(solution)/shard_map/all_gather | solution.py:39
  8.0 110.9 %reduce-scatter.6.cloned.1.call-start = ((), (), s32[]{:S(2)}) async-start(), calls=%async_computation.7 | async-start | bytes 3538944 | tf_op jit(solution)/shard_map/reduce_scatter | solution.py:47
  77.3 144.2 %all-gather.12.cloned.1.call-start = ((), (), s32[]{:S(2)}) async-start(), calls=%async_computation.14 | async-start | bytes 4718592 | tf_op jit(solution)/shard_map/all_gather | solution.py:43
  78.0 224.0 %all-reduce.2.cloned.1.call-start = ((), (), s32[]{:S(2)}) async-start(), calls=%async_computation.6 | async-start | bytes 1048576 | tf_op jit(solution)/shard_map/psum | solution.py:11
  83.2 271.2 %reduce-scatter.8.cloned.1.call-start = ((), (), s32[]{:S(2)}) async-start(), calls=%async_computation.8 | async-start | bytes 3538944 | tf_op jit(solution)/shard_map/reduce_scatter | solution.py:50
  124.3 274.2 %all-gather.14.cloned.1.call-start = ((), (), s32[]{:S(2)}) async-start(), calls=%async_computation.15 | async-start | bytes 2359296 | tf_op jit(solution)/shard_map/all_gather | solution.py:79
  124.3 230.0 %copy-start = (f32[1024,1,128]{2,1,0:T(1,128)S(1)}, f32[1024,1,128]{2,1,0:T(1,128)}, u32[]{:S(2)}) copy-start(f32[1024,1,128]{2,1,0:T(1,128)} %get-tuple-element.6) | copy-start | bytes 1572868
  304.3 145.8 %reduce-scatter.10.cloned.1.call-start = ((), (), s32[]{:S(2)}) async-start(), calls=%async_computation.9 | async-start | bytes 3538944 | tf_op jit(solution)/shard_map/reduce_scatter | solution.py:54
  359.7 187.7 %reduce-scatter.12.cloned.1.call-start = ((), (), s32[]{:S(2)}) async-start(), calls=%async_computation.10 | async-start | bytes 2162688 | tf_op jit(solution)/shard_map/reduce_scatter | solution.py:88
  401.2 1.0 copy-start.3
  401.2 48.9 %copy-start.1 = (f32[128,768]{1,0:T(8,128)S(1)}, f32[128,768]{1,0:T(8,128)}, u32[]{:S(2)}) copy-start(f32[128,768]{1,0:T(8,128)} %reduce-scatter.6.cloned.1.call-done) | copy-start | bytes 1179652
  454.2 150.8 %all-gather.8.cloned.1.call-start = ((), (), s32[]{:S(2)}) async-start(), calls=%async_computation.11 | async-start | bytes 2162688 | tf_op jit(solution)/shard_map/all_gather | solution.py:91
  608.1 30.6 %all-to-all-start = ((f32[8,2,128,256]{3,2,1,0:T(8,128)}), f32[8,2,128,256]{3,2,1,0:T(8,128)}, u32[]{:S(2)}, u32[]{:S(2)}) async-start(f32[8,2,128,256]{3,2,1,0:T(8,128)} %bitcast.64), calls=%async_computation.4 | async-start | bytes 4194304 | tf_op jit(solution)/shard_map/all_to_all | solution.py:94
  612.5 102.9 %reduce-scatter.14.cloned.1.call-start = ((), (), s32[]{:S(2)}) async-start(), calls=%async_computation.12 | async-start | bytes 6488064 | tf_op jit(solution)/shard_map/reduce_scatter | solution.py:97
  612.5 29.0 %slice-start = ((f32[12,64,2,128]{3,2,1,0:T(2,128)}), f32[11,64,2,128]{3,2,1,0:T(2,128)S(1)}, s32[]{:S(2)}) async-start(f32[12,64,2,128]{3,2,1,0:T(2,128)} %param.3), calls=%async_computation.16 | async-start | bytes 1441792 | tf_op jit(solution)/shard_map/slice | solution.py:92
  648.3 1.0 copy-start.2
  649.6 67.0 %copy-start.4 = (f32[64,256]{1,0:T(8,128)S(1)}, f32[64,256]{1,0:T(8,128)}, u32[]{:S(2)}) copy-start(f32[64,256]{1,0:T(8,128)} %reduce-scatter.12.cloned.1.call-done) | copy-start | bytes 196612
Sparse Core Ops, SparseCore 0:
  9.9 58.8 all-gather.9
  77.4 41.4 reduce-scatter.5
  120.6 100.7 all-gather.11
  224.0 78.0 all-reduce.1
  304.7 49.6 reduce-scatter.7
  356.2 42.2 all-gather.13
  401.2 48.8 reduce-scatter.9
  454.4 92.9 reduce-scatter.11
  550.3 54.6 all-gather.7
  648.5 66.8 reduce-scatter.13
